TPU v7x, 512 devices: a whole 4x8x8 slice. The times are simulated.
512 devices in a mesh: row: 64 (over x, y, core), col: 8 (over z).
Axes of the slice: x: 4, y: 8, z: 8, core: 2. Of those that a mesh axis runs over, the one named last changes fastest.
Arguments:
- grad_out: bfloat16 [2048, 12288], P('row', 'col'), may hold values from -3.5 to 3.5
- pre_act: bfloat16 [2048, 24576], P('col', 'row'), may hold values from -6 to 6
- down_weight: bfloat16 [24576, 12288], P('row', 'col'), may hold values from -0.0546875 to 0.0546875
Outputs:
- grad_pre: bfloat16 [2048, 24576], P('col', 'row')
- grad_weight: bfloat16 [24576, 12288], P('row', 'col')
All inputs are finite; a program needn't handle non-finite values.
Results may differ from a plain program's by a relative error of at most 0.015.
Values may be sent and summed in bfloat16 or wider, within the bound.
No kernel may reach another device: no remote copies, remote signals or barrier semaphores. Data moves between devices by JAX's collectives and lax.ppermute only.
A program may use at most 64 MiB of HBM per device.

v0:
```python
import jax
import jax.numpy as jnp
from jax import lax
from jax.sharding import PartitionSpec as P

coef = 0.7978845608
cubic = 0.044715


def gelu_fwd(x):
    return 0.5 * x * (1.0 + jnp.tanh(coef * (x + cubic * x * x * x)))


def gelu_grad(x):
    inner = coef * (x + cubic * x * x * x)
    tangent = jnp.tanh(inner)
    return 0.5 * (1.0 + tangent) + 0.5 * x * (1.0 - tangent * tangent) * coef * (
        1.0 + 3.0 * cubic * x * x
    )


def body(grad_out, pre_act, down_weight):
    grad_all = lax.all_gather(grad_out, "row", axis=0, tiled=True)
    pre_all = lax.all_gather(pre_act, "col", axis=0, tiled=True)
    hidden = gelu_fwd(pre_all.astype(jnp.float32)).astype(jnp.bfloat16)
    grad_weight = lax.dot_general(
        hidden, grad_all, (((0,), (0,)), ((), ())), preferred_element_type=jnp.float32
    ).astype(jnp.bfloat16)
    partial_term = lax.dot_general(
        grad_all, down_weight, (((1,), (1,)), ((), ())), preferred_element_type=jnp.float32
    )
    grad_hidden = lax.psum_scatter(
        partial_term.astype(jnp.bfloat16), "col", scatter_dimension=0, tiled=True
    ).astype(jnp.float32)
    grad_pre = (grad_hidden * gelu_grad(pre_act.astype(jnp.float32))).astype(jnp.bfloat16)
    return (grad_pre, grad_weight)


def solution(mesh):
    in_specs = (P("row", "col"), P("col", "row"), P("row", "col"))
    out_specs = (P("col", "row"), P("row", "col"))
    return jax.shard_map(body, mesh=mesh, in_specs=in_specs, out_specs=out_specs, check_vma=False)
```

profile of v0, /device:TPU:2, one launch (start us, length us, event | category | flops | bytes accessed | tf_op | source)
XLA Modules:
  0.0 197.5 jit_solution(17193629523569997921)
XLA Ops:
  7.2 0.0 copy-start
  7.2 0.0 all-gather.3.cloned.1.call-start
  7.2 0.7 all-gather.3.cloned.1.call-update
  7.9 0.0 all-gather.5.cloned.1.call-start
  8.0 0.7 all-gather.5.cloned.1.call-update
  8.7 0.0 reduce-scatter.2.cloned.1.call-start
  8.7 91.8 %all-gather.3.cloned.1.call-done = bf16[2048,1536]{1,0:T(8,128)(2,1)} async-done(((bf16[32,1536]{1,0:T(8,128)(2,1)}), bf16[2048,1536]{1,0:T(8,128)(2,1)}) %all-gather.3.cloned.1.call-update) | async-done | bytes 6291472 | tf_op jit(solution)/shard_map/all_gather | solution.py:23
  100.5 0.0 copy-done
  100.5 7.5 %convolution_convert_fusion.1 = bf16[2048,384]{1,0:T(8,128)(2,1)} fusion(bf16[2048,1536]{1,0:T(8,128)(2,1)} %all-gather.3.cloned.1.call-done, bf16[384,1536]{1,0:T(8,128)(2,1)S(1)} %copy-done), kind=kOutput, calls=%fused_computation.11 | convolution fusion | flops 2416705536 | bytes 9043968 | tf_op jit(solution)/shard_map/dot_general | solution.py:29
  108.0 0.0 reduce-scatter.2.cloned.1.call-update
  108.0 0.0 copy-start.1
  108.0 35.9 %all-gather.5.cloned.1.call-done = bf16[2048,384]{1,0:T(8,128)(2,1)} async-done(((bf16[256,384]{1,0:T(8,128)(2,1)}), bf16[2048,384]{1,0:T(8,128)(2,1)}) %all-gather.5.cloned.1.call-update) | async-done | bytes 1572880 | tf_op jit(solution)/shard_map/all_gather | solution.py:24
  143.9 7.0 %convolution_convert_fusion = bf16[384,1536]{1,0:T(8,128)(2,1)} fusion(bf16[2048,1536]{1,0:T(8,128)(2,1)} %all-gather.3.cloned.1.call-done, bf16[2048,384]{1,0:T(8,128)(2,1)} %all-gather.5.cloned.1.call-done), kind=kOutput, calls=%fused_computation.10 | convolution fusion | flops 2424373248 | bytes 9043968 | tf_op jit(solution)/shard_map/dot_general | solution.py:26
  150.9 38.2 %reduce-scatter.2.cloned.1.call-done = bf16[256,384]{1,0:T(8,128)(2,1)} async-done(((bf16[2048,384]{1,0:T(8,128)(2,1)}), bf16[256,384]{1,0:T(8,128)(2,1)}) %reduce-scatter.2.cloned.1.call-update) | async-done | bytes 196624 | tf_op jit(solution)/shard_map/reduce_scatter | solution.py:32
  189.1 0.0 copy-done.1
  189.1 1.9 fusion.17
Async XLA Ops:
  7.2 93.3 %copy-start = (bf16[384,1536]{1,0:T(8,128)(2,1)S(1)}, bf16[384,1536]{1,0:T(8,128)(2,1)}, u32[]{:S(2)}) copy-start(bf16[384,1536]{1,0:T(8,128)(2,1)} %param.5) | copy-start | bytes 3538948
  7.2 93.3 %all-gather.3.cloned.1.call-start = ((), (), s32[]{:S(2)}) async-start(), calls=%async_computation.1 | async-start | bytes 6389760 | tf_op jit(solution)/shard_map/all_gather | solution.py:23
  7.9 136.0 %all-gather.5.cloned.1.call-start = ((), (), s32[]{:S(2)}) async-start(), calls=%async_computation.3 | async-start | bytes 1769472 | tf_op jit(solution)/shard_map/all_gather | solution.py:24
  8.7 180.4 %reduce-scatter.2.cloned.1.call-start = ((), (), s32[]{:S(2)}) async-start(), calls=%async_computation.2 | async-start | bytes 1769472 | tf_op jit(solution)/shard_map/reduce_scatter | solution.py:32
  108.0 81.1 %copy-start.1 = (bf16[256,384]{1,0:T(8,128)(2,1)S(1)}, bf16[256,384]{1,0:T(8,128)(2,1)}, u32[]{:S(2)}) copy-start(bf16[256,384]{1,0:T(8,128)(2,1)} %param.4) | copy-start | bytes 589828
Sparse Core Ops, SparseCore 0:
  11.3 89.1 all-gather.2
  102.6 41.3 all-gather.4
  146.8 42.2 reduce-scatter.1
where the time goes:
time: 198 us; the launch traced here: 197 us
  waiting for transfers between devices  167 us (84%)
  matrix products  14.5 us (7%)
  between operations  13.8 us (7%)
    all_gather x1, waiting for transfers between devices, body(): grad_all = lax.all_gather(grad_out, 'row', axis=0, tiled=True)  91.8 us
    reduce_scatter x1, waiting for transfers between devices, body(): lax.psum_scatter(partial_term.astype(jnp.bfloat16), 'col', scatter_dimens...  38.2 us
    all_gather x1, waiting for transfers between devices, body(): pre_all = lax.all_gather(pre_act, 'col', axis=0, tiled=True)  35.9 us
    dot_general x1, matrix products, body(): lax.dot_general(grad_all, down_weight, (((1,), (1,)), ((), ())), preferre...  7.48 us
    dot_general x1, matrix products, body(): lax.dot_general(hidden, grad_all, (((0,), (0,)), ((), ())), preferred_ele...  6.99 us
  transfers between devices with their start and end apart: 3, of which 3 were waited for; matrix products, arithmetic and copies ran while one was open for 7% of the time, Pallas kernels for 0%

commit v1 on v0

--- a/solution.py
+++ b/solution.py
@@ -21,7 +21,10 @@
 
 def body(grad_out, pre_act, down_weight):
     grad_all = lax.all_gather(grad_out, "row", axis=0, tiled=True)
-    pre_all = lax.all_gather(pre_act, "col", axis=0, tiled=True)
+    pre_all = jnp.concatenate(
+        lax.all_to_all(jnp.stack([pre_act for _ in range(lax.axis_size("col"))]), "col", 0, 0),
+        axis=0,
+    )
     hidden = gelu_fwd(pre_all.astype(jnp.float32)).astype(jnp.bfloat16)
     grad_weight = lax.dot_general(
         hidden, grad_all, (((0,), (0,)), ((), ())), preferred_element_type=jnp.float32

time: 198 us -> 160 us (0.81)
  the two profiles are of different devices: /device:TPU:2 before, /device:TPU:4 now
where the time goes in v1:
time: 160 us; the launch traced here: 159 us
  waiting for transfers between devices  117 us (73%)
  between operations  14.1 us (9%)
  matrix products  13.9 us (9%)
  starting transfers between devices  10.4 us (6%)
  local copies, waits for them, and re-layouts  2.31 us (1%)
  other arithmetic  1.89 us (1%)
    all_gather x1, waiting for transfers between devices, body(): grad_all = lax.all_gather(grad_out, 'row', axis=0, tiled=True)  79.8 us
    reduce_scatter x1, waiting for transfers between devices, body(): lax.psum_scatter(partial_term.astype(jnp.bfloat16), 'col', scatter_dimens...  36.3 us
    all_to_all x1, starting transfers between devices, body(): lax.all_to_all(jnp.stack([pre_act for _ in range(lax.axis_size('col'))]),...  10.3 us
    dot_general x1, matrix products, body(): lax.dot_general(grad_all, down_weight, (((1,), (1,)), ((), ())), preferre...  7.38 us
    dot_general x1, matrix products, body(): lax.dot_general(hidden, grad_all, (((0,), (0,)), ((), ())), preferred_ele...  6.54 us
  transfers between devices with their start and end apart: 3, of which 2 were waited for; matrix products, arithmetic and copies ran while one was open for 10% of the time, Pallas kernels for 0%

profile of v1, /device:TPU:4, one launch (start us, length us, event | category | flops | bytes accessed | tf_op | source)
XLA Modules:
  0.0 159.3 jit_solution(14611837673106509766)
XLA Ops:
  7.2 0.0 copy-start
  7.2 0.0 all-gather.2.cloned.1.call-start
  7.2 0.7 all-gather.2.cloned.1.call-update
  7.9 2.3 %stack.2 = bf16[8,256,384]{2,1,0:T(8,128)(2,1)} broadcast(bf16[256,384]{1,0:T(8,128)(2,1)} %param.4), dimensions={1,2} | broadcast | bytes 1769472 | tf_op jit(solution)/shard_map/stack | solution.py:25
  10.2 10.3 %all-to-all-start = ((bf16[8,256,384]{2,1,0:T(8,128)(2,1)}), bf16[8,256,384]{2,1,0:T(8,128)(2,1)S(1)}, u32[]{:S(2)}, u32[]{:S(2)}) async-start(bf16[8,256,384]{2,1,0:T(8,128)(2,1)} %stack.2), calls=%async_computation.1 | async-start | bytes 3145728 | tf_op jit(solution)/shard_map/all_to_all | solution.py:25
  20.5 0.0 reduce-scatter.2.cloned.1.call-start
  20.6 79.8 %all-gather.2.cloned.1.call-done = bf16[2048,1536]{1,0:T(8,128)(2,1)} async-done(((bf16[32,1536]{1,0:T(8,128)(2,1)}), bf16[2048,1536]{1,0:T(8,128)(2,1)}) %all-gather.2.cloned.1.call-update) | async-done | bytes 6291472 | tf_op jit(solution)/shard_map/all_gather | solution.py:23
  100.3 0.0 copy-done
  100.3 7.4 %convolution_convert_fusion.1 = bf16[2048,384]{1,0:T(8,128)(2,1)} fusion(bf16[2048,1536]{1,0:T(8,128)(2,1)} %all-gather.2.cloned.1.call-done, bf16[384,1536]{1,0:T(8,128)(2,1)S(1)} %copy-done), kind=kOutput, calls=%fused_computation.11 | convolution fusion | flops 2416705536 | bytes 9043968 | tf_op jit(solution)/shard_map/dot_general | solution.py:32
  107.7 0.0 reduce-scatter.2.cloned.1.call-update
  107.7 0.0 all-to-all-done
  107.7 0.0 copy-start.1
  107.8 6.5 %convolution_convert_fusion = bf16[384,1536]{1,0:T(8,128)(2,1)} fusion(bf16[2048,1536]{1,0:T(8,128)(2,1)} %all-gather.2.cloned.1.call-done, bf16[2048,384]{1,0:T(8,128)(2,1)S(1)} %bitcast.5), kind=kOutput, calls=%fused_computation.10 | convolution fusion | flops 2424373248 | bytes 9043968 | tf_op jit(solution)/shard_map/dot_general | solution.py:29
  114.3 36.3 %reduce-scatter.2.cloned.1.call-done = bf16[256,384]{1,0:T(8,128)(2,1)} async-done(((bf16[2048,384]{1,0:T(8,128)(2,1)}), bf16[256,384]{1,0:T(8,128)(2,1)}) %reduce-scatter.2.cloned.1.call-update) | async-done | bytes 196624 | tf_op jit(solution)/shard_map/reduce_scatter | solution.py:35
  150.6 0.0 copy-done.1
  150.6 1.9 %fusion.17 = bf16[256,384]{1,0:T(8,128)(2,1)} fusion(bf16[256,384]{1,0:T(8,128)(2,1)S(1)} %copy-done.1, bf16[256,384]{1,0:T(8,128)(2,1)} %reduce-scatter.2.cloned.1.call-done), kind=kLoop, calls=%fused_computation.30 | loop fusion | flops 2064384 | bytes 589824 | tf_op jit(solution)/shard_map/convert_element_type | solution.py:38
Async XLA Ops:
  7.2 93.2 %copy-start = (bf16[384,1536]{1,0:T(8,128)(2,1)S(1)}, bf16[384,1536]{1,0:T(8,128)(2,1)}, u32[]{:S(2)}) copy-start(bf16[384,1536]{1,0:T(8,128)(2,1)} %param.5) | copy-start | bytes 3538948
  7.2 93.1 %all-gather.2.cloned.1.call-start = ((), (), s32[]{:S(2)}) async-start(), calls=%async_computation.2 | async-start | bytes 6389760 | tf_op jit(solution)/shard_map/all_gather | solution.py:23
  10.2 97.5 %all-to-all-start = ((bf16[8,256,384]{2,1,0:T(8,128)(2,1)}), bf16[8,256,384]{2,1,0:T(8,128)(2,1)S(1)}, u32[]{:S(2)}, u32[]{:S(2)}) async-start(bf16[8,256,384]{2,1,0:T(8,128)(2,1)} %stack.2), calls=%async_computation.1 | async-start | bytes 3145728 | tf_op jit(solution)/shard_map/all_to_all | solution.py:25
  20.5 130.1 %reduce-scatter.2.cloned.1.call-start = ((), (), s32[]{:S(2)}) async-start(), calls=%async_computation.3 | async-start | bytes 1769472 | tf_op jit(solution)/shard_map/reduce_scatter | solution.py:35
  107.7 42.8 %copy-start.1 = (bf16[256,384]{1,0:T(8,128)(2,1)S(1)}, bf16[256,384]{1,0:T(8,128)(2,1)}, u32[]{:S(2)}) copy-start(bf16[256,384]{1,0:T(8,128)(2,1)} %param.4) | copy-start | bytes 589828
Sparse Core Ops, SparseCore 0:
  11.3 88.9 all-gather.1
  107.9 42.6 reduce-scatter.1
